TPU v7x, 128 devices: a whole 4x4x4 slice. The times are simulated.
128 devices in a mesh: dp: 16 (over z, y_lo, core), space: 8 (over x, y_hi).
Axes of the slice: x: 4, y: 4 (y_hi: 2, y_lo: 2; y = y_hi * 2 + y_lo), z: 4, core: 2. Of those that a mesh axis runs over, the one named last changes fastest.
Arguments:
- decoder_input: bfloat16 [16, 64, 16, 16, 128], P('dp', None, 'space'), may hold values from -6 to 6
- cotangent: bfloat16 [16, 64, 16, 16, 128], P('dp', None, 'space'), may hold values from -6 to 6
- encoder_input: bfloat16 [16, 64, 16, 16, 128], P('dp', None, 'space'), may hold values from -6 to 6
- decoder_weights: bfloat16 [2, 27, 4096], replicated, may hold values from -0.15625 to 0.15625
- other_grads: bfloat16 [16, 8, 12, 27, 4096], P('dp', 'space'), may hold values from -384 to 384
- assignment: int32 [12], replicated, may hold values from 0 to 31, as said below
- moment_first: float32 [32, 27, 4096], P('dp', None, 'space'), may hold values from -4 to 4
- moment_second: float32 [32, 27, 4096], P('dp', None, 'space'), may hold values from 0.02 to 2
- master_weights: float32 [32, 27, 4096], P('dp', None, 'space'), may hold values from -0.15625 to 0.15625
Outputs:
- input_grad: bfloat16 [16, 64, 16, 16, 128], P('dp', None, 'space')
- encoder_out: bfloat16 [16, 64, 16, 16, 128], P('dp', None, 'space')
- new_params: bfloat16 [12, 27, 4096], replicated
- new_first: float32 [32, 27, 4096], P('dp', None, 'space')
- new_second: float32 [32, 27, 4096], P('dp', None, 'space')
- new_master: float32 [32, 27, 4096], P('dp', None, 'space')
Inputs may be any that keep to these rules, and one draw needn't show every extreme that they name: `assignment`: the values are distinct; value j places the tensor with owner j // 2 in that owner's slot j % 2; some owner holds 2 tensors.
All inputs are finite; a program needn't handle non-finite values.
Results may differ from a plain program's by a relative error of at most 0.005.
Values may be sent and summed in bfloat16 or wider, within the bound.
No kernel may reach another device: no remote copies, remote signals or barrier semaphores. Data moves between devices by JAX's collectives and lax.ppermute only.
A program may use at most 128 MiB of HBM per device.

v0:
```python
import math

import jax
import jax.numpy as jnp
from jax import lax
from jax.sharding import PartitionSpec as P

learn_rate = 0.002
decay_rate = 0.1
epsilon = 1e-08
bias_one = 1.0 - (0.9**50) ** 2
bias_two = 1.0 - (0.999**50) ** 2
volume_dims = ("NCDHW", "OIDHW", "NCDHW")
swapped_dims = ("CNDHW", "OIDHW", "NCDHW")


def padded_2(block, sides, width):
    for axis, dim in sides:
        count = lax.axis_size(axis)
        forward = [(i, i + 1) for i in range(count - 1)]
        forward.append((count - 1, 0))
        backward = [(target, source) for source, target in forward]
        low = lax.ppermute(
            lax.slice_in_dim(block, block.shape[dim] - width, None, axis=dim), axis, forward
        )
        high = lax.ppermute(lax.slice_in_dim(block, 0, width, axis=dim), axis, backward)
        block = jnp.concatenate([low, block, high], axis=dim)
    return block


def widened(field):
    rimmed = padded_2(field, (("space", 1),), 1)
    return jnp.pad(rimmed, ((0, 0), (0, 0), (1, 1), (1, 1)), mode="wrap")


def forward_local(padded, kernel):
    channels = kernel.shape[1]
    weights = kernel.reshape(3, 3, 3, channels, channels).transpose(3, 4, 0, 1, 2)
    result = lax.conv_general_dilated(
        padded[None],
        weights,
        (1, 1, 1),
        "VALID",
        dimension_numbers=volume_dims,
        preferred_element_type=jnp.float32,
    )
    return result[0].reshape(channels, -1)


def backward_local(padded, kernel):
    channels = kernel.shape[1]
    weights = kernel.reshape(3, 3, 3, channels, channels)[::-1, ::-1, ::-1].transpose(4, 3, 0, 1, 2)
    result = lax.conv_general_dilated(
        padded[None],
        weights,
        (1, 1, 1),
        "VALID",
        dimension_numbers=volume_dims,
        preferred_element_type=jnp.float32,
    )
    return result[0].reshape(channels, -1)


def kernel_grad(grad_field, padded):
    channels = grad_field.shape[0]
    result = lax.conv_general_dilated(
        padded[None],
        grad_field[:, None],
        (1, 1, 1),
        "VALID",
        dimension_numbers=swapped_dims,
        preferred_element_type=jnp.float32,
    )
    return result.transpose(2, 3, 4, 1, 0).reshape(27, channels, channels)


def per_device(
    decoder_input,
    cotangent,
    encoder_input,
    decoder_weights,
    other_grads,
    assignment,
    moment_first,
    moment_second,
    master_weights,
):
    field_shape = decoder_input.shape[1:]
    channels = field_shape[0]
    thick = field_shape[1]
    kernel_a = decoder_weights[0].reshape(27, channels, channels)
    kernel_b = decoder_weights[1].reshape(27, channels, channels)
    dec_field = decoder_input[0]
    dec_wide = widened(dec_field)
    preact = forward_local(dec_wide, kernel_a)
    sigma = jax.nn.sigmoid(preact)
    hidden = (preact * sigma).astype(jnp.bfloat16).reshape(field_shape)
    cot_field = cotangent[0]
    grad_b = kernel_grad(cot_field, widened(hidden))
    grad_hidden = backward_local(widened(cot_field), kernel_b)
    grad_pre = (
        (grad_hidden * sigma * (1.0 + preact * (1.0 - sigma)))
        .astype(jnp.bfloat16)
        .reshape(field_shape)
    )
    grad_a = kernel_grad(grad_pre, dec_wide)
    input_grad = backward_local(widened(grad_pre), kernel_a)
    input_grad = input_grad.astype(jnp.bfloat16).reshape((1,) + field_shape)
    replicas = lax.axis_size("dp")
    slabs = lax.axis_size("space")
    scale = 1.0 / math.sqrt(replicas * thick * slabs * field_shape[2] * field_shape[3])
    local_grads = other_grads[0, 0].astype(jnp.float32)
    local_grads = local_grads.at[0].add(grad_a.reshape(27, -1))
    local_grads = local_grads.at[1].add(grad_b.reshape(27, -1))
    local_grads = local_grads * scale
    slot_count = moment_first.shape[0]
    every_slot = replicas * slot_count
    padded_grads = (
        jnp.zeros((every_slot,) + local_grads.shape[1:], jnp.float32)
        .at[assignment]
        .set(local_grads)
    )
    owned_full = lax.psum_scatter(
        padded_grads.astype(jnp.bfloat16), "dp", scatter_dimension=0, tiled=True
    )
    owned = lax.psum_scatter(owned_full, "space", scatter_dimension=2, tiled=True).astype(
        jnp.float32
    )
    new_first = 0.9 * moment_first + 0.1 * owned
    new_second = 0.999 * moment_second + 0.001 * owned * owned
    update = new_first / bias_one / (jnp.sqrt(new_second / bias_two) + epsilon)
    new_master = master_weights - learn_rate * (update + decay_rate * master_weights)
    mine_rounded = new_master.astype(jnp.bfloat16)
    gathered = lax.all_gather(mine_rounded, "dp", axis=0, tiled=True)
    picked = jnp.take(gathered, assignment, axis=0)
    new_params = lax.all_gather(picked, "space", axis=2, tiled=True)
    kernel_c = new_params[2].reshape(27, channels, channels)
    kernel_d = new_params[3].reshape(27, channels, channels)
    enc_field = encoder_input[0]
    first = forward_local(widened(enc_field), kernel_c)
    activ = (first * jax.nn.sigmoid(first)).astype(jnp.bfloat16).reshape(field_shape)
    second = forward_local(widened(activ), kernel_d)
    encoder_out = (enc_field.reshape(channels, -1).astype(jnp.float32) + second).astype(
        jnp.bfloat16
    )
    encoder_out = encoder_out.reshape((1,) + field_shape)
    return (input_grad, encoder_out, new_params, new_first, new_second, new_master)


def solution(mesh):
    in_specs = (
        P("dp", None, "space", None, None),
        P("dp", None, "space", None, None),
        P("dp", None, "space", None, None),
        P(),
        P("dp", "space", None, None, None),
        P(),
        P("dp", None, "space"),
        P("dp", None, "space"),
        P("dp", None, "space"),
    )
    out_specs = (
        P("dp", None, "space", None, None),
        P("dp", None, "space", None, None),
        P(),
        P("dp", None, "space"),
        P("dp", None, "space"),
        P("dp", None, "space"),
    )
    return jax.shard_map(
        per_device, mesh=mesh, in_specs=in_specs, out_specs=out_specs, check_vma=False
    )
```

profile of v0, /device:TPU:0, one launch (start us, length us, event | category | flops | bytes accessed | tf_op | source)
XLA Modules:
  0.0 589.0 jit_solution(8464938138761294189)
XLA Ops:
  21.7 6.1 %fusion.104 = (f32[1,1,12,27,4096]{4,3,2,1,0:T(8,128)}, f32[12,27,4096]{2,1,0:T(8,128)}) fusion(bf16[1,1,12,27,4096]{4,3,2,1,0:T(8,128)(2,1)S(1)} %copy-done.13), kind=kLoop, calls=%fused_computation.149 | loop fusion | flops 1327104 | bytes 13271040 | tf_op jit(solution)/shard_map/convert_element_type | solution.py:112
  40.4 5.9 copy.161
  50.2 8.6 %fusion.50 = f32[2,16,8,17,64]{4,2,3,1,0:T(8,128)S(1)} fusion(bf16[3,3,3,64,64]{4,3,2,1,0:T(8,128)(2,1)S(1)} %copy-done.20, bf16[64,4,18,1,7,2]{0,4,5,2,1,3:T(8,128)(2,1)S(1)} %slice.233, bf16[64,4,18,1,8,17]{0,4,5,2,1,3:T(8,128)(2,1)S(1)} %copy.115, pred[8,17]{0,1:T(8,128)(4,1)S(1)} %copy-done.28), kind=kOutput, calls=%fused_computation.54 | convolution fusion | flops 967073792 | bytes 2717832 | tf_op jit(solution)/shard_map/conv_general_dilated | solution.py:39
  68.9 6.4 %maximum_bitcast_fusion = bf16[64,4,18,1,130]{4,2,1,0,3:T(8,128)(2,1)} fusion(bf16[64,4,18,1]{3,2,1,0:T(8,128)(2,1)S(1)} %get-tuple-element.67, bf16[64,4,1,128]{3,2,1,0:T(2,128)(2,1)S(1)} %get-tuple-element.89, bf16[64,1,16,128]{3,2,1,0:T(8,128)(2,1)} %collective-permute-done.1, bf16[64,2,16,128]{3,2,1,0:T(8,128)(2,1)S(1)} %bitcast.163, ...), kind=kLoop, calls=%fused_computation.8 | loop fusion | flops 8386560 | bytes 2396160 | tf_op jit(solution)/shard_map/broadcast_in_dim | solution.py:54
  75.3 8.0 %copy.160 = bf16[64,4,18,1,130]{0,1,4,2,3:T(4,128)(2,1)} copy(bf16[64,4,18,1,130]{4,2,1,0,3:T(8,128)(2,1)} %maximum_bitcast_fusion) | data formatting | bytes 2396160
  105.2 12.2 %copy.131 = bf16[1,64,4,18,130]{1,0,4,3,2:T(2,128)(2,1)} copy(bf16[1,64,4,18,130]{4,1,3,2,0:T(8,128)(2,1)} %fusion.131) | data formatting | bytes 2396160 | tf_op jit(solution)/shard_map/broadcast_in_dim | solution.py:40
  118.7 33.1 %fusion.120 = f32[3,3,3,64,64]{4,3,2,1,0:T(8,128)} fusion(bf16[1,64,4,18,130]{1,0,4,3,2:T(2,128)(2,1)} %copy.131, bf16[64,1,2,16,128]{0,1,4,3,2:T(2,128)(2,1)S(1)} %copy.132), kind=kOutput, calls=%fused_computation.165 | convolution fusion | flops 905969664 | bytes 2164736 | tf_op jit(solution)/shard_map/transpose | solution.py:74
  153.3 5.7 collective-permute-start.9
  163.5 5.8 collective-permute-done.8
  172.3 9.1 %copy.137 = bf16[1,64,4,18,130]{1,0,4,3,2:T(2,128)(2,1)} copy(bf16[1,64,4,18,130]{4,1,3,2,0:T(8,128)(2,1)S(1)} %maximum_bitcast_fusion.3) | data formatting | bytes 2396160 | tf_op jit(solution)/shard_map/broadcast_in_dim | solution.py:67
  181.5 32.9 %fusion.121 = f32[3,3,3,64,64]{4,3,2,1,0:T(8,128)S(1)} fusion(bf16[1,64,4,18,130]{1,0,4,3,2:T(2,128)(2,1)} %copy.137, bf16[64,1,2,16,128]{0,1,4,3,2:T(2,128)(2,1)} %copy.138), kind=kOutput, calls=%fused_computation.166 | convolution fusion | flops 905969664 | bytes 2164736 | tf_op jit(solution)/shard_map/transpose | solution.py:74
  216.6 6.4 %broadcast_multiply_fusion = f32[12,27,4096]{2,1,0:T(8,128)} fusion(f32[12,27,4096]{2,1,0:T(8,128)} %fusion.78), kind=kLoop, calls=%fused_computation.10 | loop fusion | flops 1327104 | bytes 10616832 | tf_op jit(solution)/shard_map/mul | solution.py:115
  223.0 7.9 %broadcast_in_dim.40 = f32[32,27,4096]{2,1,0:T(8,128)} broadcast(f32[]{:T(128)} %constant.85.clone.1), dimensions={} | broadcast | bytes 14155780 | tf_op jit(solution)/shard_map/broadcast_in_dim | solution.py:119
  230.9 11.7 %scatter_fusion = f32[32,27,4096]{2,1,0:T(8,128)} fusion(f32[32,27,4096]{2,1,0:T(8,128)} %broadcast_in_dim.40, s32[12]{0:T(128)S(1)} %compare_select_fusion, f32[12,27,4096]{2,1,0:T(8,128)} %broadcast_multiply_fusion), kind=kCustom, calls=%fused_computation.1 | custom fusion | bytes 15925296 | tf_op jit(solution)/shard_map/scatter | solution.py:121
  242.6 9.0 %convert_element_type.55 = bf16[32,27,4096]{2,1,0:T(8,128)(2,1)} convert(f32[32,27,4096]{2,1,0:T(8,128)} %scatter_fusion) | non-fusion elementwise | flops 3538944 | bytes 21233664 | tf_op jit(solution)/shard_map/convert_element_type | solution.py:124
  251.7 98.6 %reduce-scatter.3.cloned.1.call-done = bf16[2,27,4096]{2,1,0:T(8,128)(2,1)} async-done(((bf16[32,27,4096]{2,1,0:T(8,128)(2,1)}), bf16[2,27,4096]{2,1,0:T(8,128)(2,1)}) %reduce-scatter.3.cloned.1.call-update) | async-done | bytes 442384 | tf_op jit(solution)/shard_map/reduce_scatter | solution.py:123
  350.4 73.6 %reduce-scatter.5.cloned.1.call-done = bf16[2,27,512]{2,1,0:T(8,128)(2,1)} async-done(((bf16[2,27,4096]{2,1,0:T(8,128)(2,1)}), bf16[2,27,512]{2,1,0:T(8,128)(2,1)}) %reduce-scatter.5.cloned.1.call-update) | async-done | bytes 55312 | tf_op jit(solution)/shard_map/reduce_scatter | solution.py:126
  425.7 24.4 %all_gather.6 = bf16[32,27,512]{2,1,0:T(8,128)(2,1)S(1)} all-gather(bf16[2,27,512]{2,1,0:T(8,128)(2,1)S(1)} %get-tuple-element.56), channel_id=1, replica_groups=mesh['dp'=16,'space'=8] {'dp'}, dimensions={0}, use_global_device_ids=true | all-gather | bytes 940032 | tf_op jit(solution)/shard_map/all_gather | solution.py:134
  467.4 9.5 %collective-permute-done.6 = bf16[64,1,16,128]{3,2,1,0:T(8,128)(2,1)S(1)} collective-permute-done((bf16[64,1,16,128]{3,2,1,0:T(8,128)(2,1)S(1)}, bf16[64,1,16,128]{3,2,1,0:T(8,128)(2,1)S(1)}, u32[]{:S(2)}, u32[]{:S(2)}) %collective-permute-start.6) | collective-permute-done | bytes 262176 | tf_op jit(solution)/shard_map/ppermute | solution.py:23
  484.2 7.8 %copy.162 = bf16[64,4,18,1,130]{0,1,4,2,3:T(4,128)(2,1)S(1)} copy(bf16[64,4,18,1,130]{4,2,1,0,3:T(8,128)(2,1)} %maximum_bitcast_fusion.1) | data formatting | bytes 2396160
  511.7 11.2 %all-gather.2.cloned.1.call-done = bf16[12,27,4096]{2,1,0:T(8,128)(2,1)} async-done(((bf16[12,27,512]{2,1,0:T(8,128)(2,1)}), bf16[12,27,4096]{2,1,0:T(8,128)(2,1)}) %all-gather.2.cloned.1.call-update) | async-done | bytes 2654224 | tf_op jit(solution)/shard_map/all_gather | solution.py:136
  524.5 10.5 %fusion.47 = f32[2,16,8,17,64]{4,2,3,1,0:T(8,128)S(1)} fusion(bf16[3,3,3,64,64]{4,3,2,1,0:T(8,128)(2,1)S(1)} %reshape_reshape_squeeze.15, bf16[64,4,18,1,7,2]{0,4,5,2,1,3:T(8,128)(2,1)S(1)} %copy-done.23, bf16[64,4,18,1,8,17]{0,4,5,2,1,3:T(8,128)(2,1)} %copy-done.14, pred[8,17]{0,1:T(8,128)(4,1)S(1)} %copy-done.28), kind=kOutput, calls=%fused_computation.53 | convolution fusion | flops 967073792 | bytes 2717832 | tf_op jit(solution)/shard_map/conv_general_dilated | solution.py:39
  548.6 5.7 collective-permute-done.11
  566.2 8.6 %fusion.42 = f32[2,16,8,17,64]{4,2,3,1,0:T(8,128)S(1)} fusion(bf16[3,3,3,64,64]{4,3,2,1,0:T(8,128)(2,1)S(1)} %reshape_reshape_squeeze.16, bf16[64,4,18,1,7,2]{0,4,5,2,1,3:T(8,128)(2,1)S(1)} %slice.264, bf16[64,4,18,1,8,17]{0,4,5,2,1,3:T(8,128)(2,1)S(1)} %copy.150, pred[8,17]{0,1:T(8,128)(4,1)S(1)} %copy-done.28), kind=kOutput, calls=%fused_computation.52 | convolution fusion | flops 967073792 | bytes 2717832 | tf_op jit(solution)/shard_map/conv_general_dilated | solution.py:39
  (184 shorter events, 155.7 us)
Async XLA Ops:
  7.2 343.2 %reduce-scatter.3.cloned.1.call-start = ((), (), s32[]{:S(2)}) async-start(), calls=%async_computation.2 | async-start | bytes 8912896 | tf_op jit(solution)/shard_map/reduce_scatter | solution.py:123
  7.2 14.5 %copy-start.13 = (bf16[1,1,12,27,4096]{4,3,2,1,0:T(8,128)(2,1)S(1)}, bf16[1,1,12,27,4096]{4,3,2,1,0:T(8,128)(2,1)}, u32[]{:S(2)}) copy-start(bf16[1,1,12,27,4096]{4,3,2,1,0:T(8,128)(2,1)} %param.17) | copy-start | bytes 7962628
  8.7 26.1 %collective-permute-start.3 = (bf16[64,1,16,128]{3,0,2,1:T(8,128)(2,1)S(1)}, bf16[64,1,16,128]{3,0,2,1:T(8,128)(2,1)S(1)}, u32[]{:S(2)}, u32[]{:S(2)}) collective-permute-start(bf16[64,1,16,128]{3,0,2,1:T(8,128)(2,1)S(1)} %get-tuple-element.99), channel_id=1, source_target_pairs={{1,0},{2,1},{3,2},{4,3},{5,4},{6,5},{7,6},{0,7},{9,8},{10,9},{11,1... | collective-permute-start | bytes 786440 | tf_op jit(solution)/shard_map/ppermute | solution.py:26
  14.2 20.5 %collective-permute-start.2 = (bf16[64,1,16,128]{3,0,2,1:T(8,128)(2,1)S(1)}, bf16[64,1,16,128]{3,0,2,1:T(8,128)(2,1)S(1)}, u32[]{:S(2)}, u32[]{:S(2)}) collective-permute-start(bf16[64,1,16,128]{3,0,2,1:T(8,128)(2,1)S(1)} %get-tuple-element.98), channel_id=1, source_target_pairs={{0,1},{1,2},{2,3},{3,4},{4,5},{5,6},{6,7},{7,0},{8,9},{9,10},{10,1... | collective-permute-start | bytes 786440 | tf_op jit(solution)/shard_map/ppermute | solution.py:23
  16.1 48.4 %collective-permute-start.1 = (bf16[64,1,16,128]{3,2,1,0:T(8,128)(2,1)}, bf16[64,1,16,128]{3,2,1,0:T(8,128)(2,1)}, u32[]{:S(2)}, u32[]{:S(2)}) collective-permute-start(bf16[64,1,16,128]{3,2,1,0:T(8,128)(2,1)} %get-tuple-element.101), channel_id=1, source_target_pairs={{1,0},{2,1},{3,2},{4,3},{5,4},{6,5},{7,6},{0,7},{9,8},{10,9},{11,1... | collective-permute-start | bytes 786440 | tf_op jit(solution)/shard_map/ppermute | solution.py:26
  21.7 42.7 %collective-permute-start = (bf16[64,1,16,128]{3,2,1,0:T(8,128)(2,1)}, bf16[64,1,16,128]{3,2,1,0:T(8,128)(2,1)}, u32[]{:S(2)}, u32[]{:S(2)}) collective-permute-start(bf16[64,1,16,128]{3,2,1,0:T(8,128)(2,1)} %get-tuple-element.100), channel_id=1, source_target_pairs={{0,1},{1,2},{2,3},{3,4},{4,5},{5,6},{6,7},{7,0},{8,9},{9,10},{10,1... | collective-permute-start | bytes 786440 | tf_op jit(solution)/shard_map/ppermute | solution.py:23
  105.2 12.2 %copy-start.15 = (bf16[64,1,2,16,128]{4,3,2,1,0:T(8,128)(2,1)S(1)}, bf16[64,1,2,16,128]{4,3,2,1,0:T(8,128)(2,1)}, u32[]{:S(2)}) copy-start(bf16[64,1,2,16,128]{4,3,2,1,0:T(8,128)(2,1)} %fusion.62) | copy-start | bytes 1572868
  153.3 10.2 %collective-permute-start.9 = (bf16[64,1,16,128]{3,2,1,0:T(8,128)(2,1)S(1)}, bf16[64,1,16,128]{3,2,1,0:T(8,128)(2,1)S(1)}, u32[]{:S(2)}, u32[]{:S(2)}) collective-permute-start(bf16[64,1,16,128]{3,2,1,0:T(8,128)(2,1)S(1)} %get-tuple-element.95), channel_id=1, source_target_pairs={{1,0},{2,1},{3,2},{4,3},{5,4},{6,5},{7,6},{0,7},{9,8},{10,9},{11,1... | collective-permute-start | bytes 786440 | tf_op jit(solution)/shard_map/ppermute | solution.py:26
  159.0 10.3 %collective-permute-start.8 = (bf16[64,1,16,128]{3,2,1,0:T(8,128)(2,1)S(1)}, bf16[64,1,16,128]{3,2,1,0:T(8,128)(2,1)S(1)}, u32[]{:S(2)}, u32[]{:S(2)}) collective-permute-start(bf16[64,1,16,128]{3,2,1,0:T(8,128)(2,1)S(1)} %get-tuple-element.94), channel_id=1, source_target_pairs={{0,1},{1,2},{2,3},{3,4},{4,5},{5,6},{6,7},{7,0},{8,9},{9,10},{10,1... | collective-permute-start | bytes 786440 | tf_op jit(solution)/shard_map/ppermute | solution.py:23
  251.6 172.4 %copy-start.24 = (f32[2,27,512]{2,0,1:T(2,128)S(1)}, f32[2,27,512]{2,0,1:T(2,128)}, u32[]{:S(2)}) copy-start(f32[2,27,512]{2,0,1:T(2,128)} %param.21) | copy-start | bytes 331780
  251.6 172.4 %copy-start.25 = (f32[2,27,512]{2,0,1:T(2,128)S(1)}, f32[2,27,512]{2,0,1:T(2,128)}, u32[]{:S(2)}) copy-start(f32[2,27,512]{2,0,1:T(2,128)} %param.19) | copy-start | bytes 331780
  251.6 172.4 %copy-start.26 = (f32[2,27,512]{2,0,1:T(2,128)S(1)}, f32[2,27,512]{2,0,1:T(2,128)}, u32[]{:S(2)}) copy-start(f32[2,27,512]{2,0,1:T(2,128)} %param.20) | copy-start | bytes 331780
  251.7 199.8 %copy-start.1 = (bf16[1,64,2,16,128]{4,3,2,1,0:T(8,128)(2,1)S(1)}, bf16[1,64,2,16,128]{4,3,2,1,0:T(8,128)(2,1)}, u32[]{:S(2)}) copy-start(bf16[1,64,2,16,128]{4,3,2,1,0:T(8,128)(2,1)} %param.15) | copy-start | bytes 1572868
  251.7 172.4 %reduce-scatter.5.cloned.1.call-start = ((), (), s32[]{:S(2)}) async-start(), calls=%async_computation.3 | async-start | bytes 589824 | tf_op jit(solution)/shard_map/reduce_scatter | solution.py:126
  350.4 172.6 %all-gather.2.cloned.1.call-start = ((), (), s32[]{:S(2)}) async-start(), calls=%async_computation.4 | async-start | bytes 3538944 | tf_op jit(solution)/shard_map/all_gather | solution.py:136
  451.6 15.9 %collective-permute-start.7 = (bf16[64,1,16,128]{3,2,1,0:T(8,128)(2,1)S(1)}, bf16[64,1,16,128]{3,2,1,0:T(8,128)(2,1)S(1)}, u32[]{:S(2)}, u32[]{:S(2)}) collective-permute-start(bf16[64,1,16,128]{3,2,1,0:T(8,128)(2,1)S(1)} %get-tuple-element.93), channel_id=1, source_target_pairs={{1,0},{2,1},{3,2},{4,3},{5,4},{6,5},{7,6},{0,7},{9,8},{10,9},{11,1... | collective-permute-start | bytes 786440 | tf_op jit(solution)/shard_map/ppermute | solution.py:26
  455.0 21.9 %collective-permute-start.6 = (bf16[64,1,16,128]{3,2,1,0:T(8,128)(2,1)S(1)}, bf16[64,1,16,128]{3,2,1,0:T(8,128)(2,1)S(1)}, u32[]{:S(2)}, u32[]{:S(2)}) collective-permute-start(bf16[64,1,16,128]{3,2,1,0:T(8,128)(2,1)S(1)} %get-tuple-element.92), channel_id=1, source_target_pairs={{0,1},{1,2},{2,3},{3,4},{4,5},{5,6},{6,7},{7,0},{8,9},{9,10},{10,1... | collective-permute-start | bytes 786440 | tf_op jit(solution)/shard_map/ppermute | solution.py:23
  457.4 37.1 %collective-permute-start.5 = (bf16[64,1,16,128]{3,2,1,0:T(8,128)(2,1)S(1)}, bf16[64,1,16,128]{3,2,1,0:T(8,128)(2,1)}, u32[]{:S(2)}, u32[]{:S(2)}) collective-permute-start(bf16[64,1,16,128]{3,2,1,0:T(8,128)(2,1)S(1)} %get-tuple-element.97), channel_id=1, source_target_pairs={{1,0},{2,1},{3,2},{4,3},{5,4},{6,5},{7,6},{0,7},{9,8},{10,9},{11,1... | collective-permute-start | bytes 786440 | tf_op jit(solution)/shard_map/ppermute | solution.py:26
  462.9 31.5 %collective-permute-start.4 = (bf16[64,1,16,128]{3,2,1,0:T(8,128)(2,1)S(1)}, bf16[64,1,16,128]{3,2,1,0:T(8,128)(2,1)}, u32[]{:S(2)}, u32[]{:S(2)}) collective-permute-start(bf16[64,1,16,128]{3,2,1,0:T(8,128)(2,1)S(1)} %get-tuple-element.96), channel_id=1, source_target_pairs={{0,1},{1,2},{2,3},{3,4},{4,5},{5,6},{6,7},{7,0},{8,9},{9,10},{10,1... | collective-permute-start | bytes 786440 | tf_op jit(solution)/shard_map/ppermute | solution.py:23
  511.6 12.9 %copy-start.23 = (bf16[64,4,18,1,7,2]{0,4,5,2,1,3:T(8,128)(2,1)S(1)}, bf16[64,4,18,1,7,2]{0,4,5,2,1,3:T(8,128)(2,1)}, u32[]{:S(2)}) copy-start(bf16[64,4,18,1,7,2]{0,4,5,2,1,3:T(8,128)(2,1)} %slice.247) | copy-start | bytes 387076
  539.3 7.4 %copy-start.18 = (f32[2,27,512]{2,1,0:T(8,128)S(1)}, f32[2,27,512]{2,1,0:T(8,128)}, u32[]{:S(2)}) copy-start(f32[2,27,512]{2,1,0:T(8,128)} %get-tuple-element.59) | copy-start | bytes 331780
  539.3 8.1 %copy-start.17 = (f32[2,27,512]{2,1,0:T(8,128)S(1)}, f32[2,27,512]{2,1,0:T(8,128)}, u32[]{:S(2)}) copy-start(f32[2,27,512]{2,1,0:T(8,128)} %get-tuple-element.57) | copy-start | bytes 331780
  540.2 14.1 %collective-permute-start.11 = (bf16[64,1,16,128]{3,2,1,0:T(8,128)(2,1)}, bf16[64,1,16,128]{3,2,1,0:T(8,128)(2,1)}, u32[]{:S(2)}, u32[]{:S(2)}) collective-permute-start(bf16[64,1,16,128]{3,2,1,0:T(8,128)(2,1)} %get-tuple-element.91), channel_id=1, source_target_pairs={{1,0},{2,1},{3,2},{4,3},{5,4},{6,5},{7,6},{0,7},{9,8},{10,9},{11,1... | collective-permute-start | bytes 786440 | tf_op jit(solution)/shard_map/ppermute | solution.py:26
  542.5 11.8 %collective-permute-start.10 = (bf16[64,1,16,128]{3,2,1,0:T(8,128)(2,1)}, bf16[64,1,16,128]{3,2,1,0:T(8,128)(2,1)}, u32[]{:S(2)}, u32[]{:S(2)}) collective-permute-start(bf16[64,1,16,128]{3,2,1,0:T(8,128)(2,1)} %get-tuple-element.90), channel_id=1, source_target_pairs={{0,1},{1,2},{2,3},{3,4},{4,5},{5,6},{6,7},{7,0},{8,9},{9,10},{10,1... | collective-permute-start | bytes 786440 | tf_op jit(solution)/shard_map/ppermute | solution.py:23
  (20 other events, 61.3 us)
Sparse Core Ops, SparseCore 0:
  251.8 98.4 reduce-scatter.2
  353.9 70.0 reduce-scatter.4
  451.6 71.2 all-gather.1
where the time goes:
time: 597 us; the launch traced here: 589 us
  waiting for transfers between devices  211 us (35%)
  local copies, waits for them, and re-layouts  138 us (23%)
  matrix products  103 us (17%)
  other arithmetic  68.3 us (11%)
  starting transfers between devices  29.7 us (5%)
  blocking collectives  24.4 us (4%)
  between operations  14.7 us (2%)
    reduce_scatter x1, waiting for transfers between devices, per_device(): lax.psum_scatter(padded_grads.astype(jnp.bfloat16), 'dp', scatter_dimensi...  98.6 us
    reduce_scatter x1, waiting for transfers between devices, per_device(): lax.psum_scatter(owned_full, 'space', scatter_dimension=2, tiled=True)  73.6 us
    transpose x2, matrix products, kernel_grad(): return result.transpose(2, 3, 4, 1, 0).reshape(27, channels, channels)  66 us
    unnamed x80, local copies, waits for them, and re-layouts  59.9 us
    ppermute x6, starting transfers between devices, padded_2(): lax.ppermute(lax.slice_in_dim(block, 0, width, axis=dim), axis, backward)  28.3 us
    conv_general_dilated x3, matrix products, forward_local(): lax.conv_general_dilated(padded[None], weights, (1, 1, 1), 'VALID', dimen...  27.7 us
    all_gather x1, blocking collectives, per_device(): gathered = lax.all_gather(mine_rounded, 'dp', axis=0, tiled=True)  24.4 us
    broadcast_in_dim x4, local copies, waits for them, and re-layouts, forward_local(): padded[None]  17.7 us
  transfers between devices with their start and end apart: 15, of which 8 were waited for; matrix products, arithmetic and copies ran while one was open for 15% of the time, Pallas kernels for 0%

commit v1 on v0

--- a/solution.py
+++ b/solution.py
@@ -72,6 +72,39 @@
         preferred_element_type=jnp.float32,
     )
     return result.transpose(2, 3, 4, 1, 0).reshape(27, channels, channels)
+
+
+def space_scatter(block):
+    count = lax.axis_size("space")
+    lead = block.shape[:-1]
+    split = block.reshape(lead + (count, block.shape[-1] // count))
+    split = jnp.moveaxis(split, -2, 0)
+    return lax.psum_scatter(split, "space", scatter_dimension=0, tiled=True)[0]
+
+
+def space_gather(block):
+    count = lax.axis_size("space")
+    lead = block.shape[:-1]
+    whole = lax.all_gather(block, "space", axis=0, tiled=False)
+    whole = jnp.moveaxis(whole, 0, -2)
+    return whole.reshape(lead + (count * block.shape[-1],))
+
+
+def adamw(grads, first, second, master):
+    new_first = 0.9 * first + 0.1 * grads
+    new_second = 0.999 * second + 0.001 * grads * grads
+    update = new_first / bias_one / (jnp.sqrt(new_second / bias_two) + epsilon)
+    new_master = master - learn_rate * (update + decay_rate * master)
+    return new_first, new_second, new_master
+
+
+def owner_rows(grads, assign, owner, first, second, master):
+    slot_count = first.shape[0]
+    local = assign % slot_count
+    pick = lambda state: jnp.take(state, local, axis=0)
+    rows = adamw(grads, pick(first), pick(second), pick(master))[2].astype(jnp.bfloat16)
+    mine = (assign // slot_count == owner)[:, None, None]
+    return jnp.where(mine, rows, jnp.zeros_like(rows))
 
 
 def per_device(
@@ -109,33 +142,30 @@
     replicas = lax.axis_size("dp")
     slabs = lax.axis_size("space")
     scale = 1.0 / math.sqrt(replicas * thick * slabs * field_shape[2] * field_shape[3])
-    local_grads = other_grads[0, 0].astype(jnp.float32)
-    local_grads = local_grads.at[0].add(grad_a.reshape(27, -1))
-    local_grads = local_grads.at[1].add(grad_b.reshape(27, -1))
-    local_grads = local_grads * scale
+    owner = lax.axis_index("dp")
+    other_tot = lax.psum(space_scatter(other_grads[0, 0]), "dp").astype(jnp.float32)
+    enc_rows = owner_rows(
+        other_tot[2:4] * scale, assignment[2:4], owner, moment_first, moment_second, master_weights
+    )
+    enc_params = space_gather(lax.psum(enc_rows, "dp"))
+    kernel_c = enc_params[0].reshape(27, channels, channels)
+    kernel_d = enc_params[1].reshape(27, channels, channels)
+    ab_grads = jnp.stack([grad_a.reshape(27, -1), grad_b.reshape(27, -1)]).astype(jnp.bfloat16)
+    ab_tot = lax.psum(space_scatter(ab_grads), "dp").astype(jnp.float32)
+    totals = jnp.concatenate([other_tot[:2] + ab_tot, other_tot[2:]]) * scale
     slot_count = moment_first.shape[0]
-    every_slot = replicas * slot_count
-    padded_grads = (
-        jnp.zeros((every_slot,) + local_grads.shape[1:], jnp.float32)
-        .at[assignment]
-        .set(local_grads)
-    )
-    owned_full = lax.psum_scatter(
-        padded_grads.astype(jnp.bfloat16), "dp", scatter_dimension=0, tiled=True
-    )
-    owned = lax.psum_scatter(owned_full, "space", scatter_dimension=2, tiled=True).astype(
-        jnp.float32
-    )
-    new_first = 0.9 * moment_first + 0.1 * owned
-    new_second = 0.999 * moment_second + 0.001 * owned * owned
-    update = new_first / bias_one / (jnp.sqrt(new_second / bias_two) + epsilon)
-    new_master = master_weights - learn_rate * (update + decay_rate * master_weights)
-    mine_rounded = new_master.astype(jnp.bfloat16)
-    gathered = lax.all_gather(mine_rounded, "dp", axis=0, tiled=True)
-    picked = jnp.take(gathered, assignment, axis=0)
-    new_params = lax.all_gather(picked, "space", axis=2, tiled=True)
-    kernel_c = new_params[2].reshape(27, channels, channels)
-    kernel_d = new_params[3].reshape(27, channels, channels)
+    slot_ids = owner * slot_count + jnp.arange(slot_count)
+    match = assignment[None, :] == slot_ids[:, None]
+    owned = jnp.sum(jnp.where(match[:, :, None, None], totals[None], 0.0), axis=1)
+    new_first, new_second, new_master = adamw(owned, moment_first, moment_second, master_weights)
+    late = jnp.array([0, 1] + list(range(4, assignment.shape[0])))
+    late_assign = assignment[late]
+    late_local = jnp.take(new_master.astype(jnp.bfloat16), late_assign % slot_count, axis=0)
+    late_rows = jnp.where(
+        (late_assign // slot_count == owner)[:, None, None], late_local, jnp.zeros_like(late_local)
+    )
+    late_params = space_gather(lax.psum(late_rows, "dp"))
+    new_params = jnp.concatenate([late_params[:2], enc_params, late_params[2:]])
     enc_field = encoder_input[0]
     first = forward_local(widened(enc_field), kernel_c)
     activ = (first * jax.nn.sigmoid(first)).astype(jnp.bfloat16).reshape(field_shape)

time: 597 us -> 797 us (1.34)
  waiting for transfers between devices: 211 us -> 395 us
  other arithmetic: 68.3 us -> 54.6 us
  local copies, waits for them, and re-layouts: 138 us -> 150 us
  blocking collectives: 24.4 us -> 34.9 us
    psum x0 -> x3, waiting for transfers between devices: none -> 309 us  [the longest x1 117 us: per_device(): lax.psum(space_scatter(other_grads[0, 0]), 'dp').astype(jnp.float32)]
    reduce_scatter x2 -> x1, waiting for transfers between devices: 172 us -> 0.02 us  [space_scatter(): return lax.psum_scatter(split, 'space', scatter_dimension=0, tiled=True)[0]]
    unnamed x3 -> x7, waiting for transfers between devices: 0.05 us -> 72.6 us
    convert_element_type x3 -> x2, other arithmetic: 16.8 us -> 1.23 us  [the longest x1 1.08 us: per_device(): lax.psum(space_scatter(other_grads[0, 0]), 'dp').astype(jnp.float32)]
    ppermute x6, waiting for transfers between devices: 15.3 us -> 0.71 us  [padded_2(): lax.ppermute(lax.slice_in_dim(block, block.shape[dim] - width, None, axis...]
    another operation x2 -> x6, local copies, waits for them, and re-layouts: 1.82 us -> 13.7 us  [the longest x2 9.21 us: space_scatter(): split = block.reshape(lead + (count, block.shape[-1] // count))]
    scatter x1 -> x0, local copies, waits for them, and re-layouts: 11.7 us -> none  [per_device(): padded_grads = jnp.zeros((every_slot,) + local_grads.shape[1:], jnp.float...]
    all_gather x1, blocking collectives: 24.4 us -> 34.9 us  [space_gather(): whole = lax.all_gather(block, 'space', axis=0, tiled=False)]
  transfers between devices with their start and end apart: 15 -> 18, of which waited for: 8 -> 7; matrix products, arithmetic and copies ran while one was open for 15% -> 36% of each run, Pallas kernels for 0% -> 0%
where the time goes in v1:
time: 797 us; the launch traced here: 786 us
  waiting for transfers between devices  395 us (50%)
  local copies, waits for them, and re-layouts  150 us (19%)
  matrix products  101 us (13%)
  other arithmetic  54.6 us (7%)
  blocking collectives  34.9 us (4%)
  starting transfers between devices  34.5 us (4%)
  between operations  15.6 us (2%)
    psum x1, waiting for transfers between devices, per_device(): lax.psum(space_scatter(other_grads[0, 0]), 'dp').astype(jnp.float32)  117 us
    psum x1, waiting for transfers between devices, per_device(): enc_params = space_gather(lax.psum(enc_rows, 'dp'))  112 us
    psum x1, waiting for transfers between devices, per_device(): late_params = space_gather(lax.psum(late_rows, 'dp'))  79.7 us
    unnamed x7, waiting for transfers between devices  72.6 us
    transpose x2, matrix products, kernel_grad(): return result.transpose(2, 3, 4, 1, 0).reshape(27, channels, channels)  63.5 us
    unnamed x116, local copies, waits for them, and re-layouts  60.2 us
    all_gather x1, blocking collectives, space_gather(): whole = lax.all_gather(block, 'space', axis=0, tiled=False)  34.9 us
    conv_general_dilated x3, matrix products, forward_local(): lax.conv_general_dilated(padded[None], weights, (1, 1, 1), 'VALID', dimen...  27.5 us
  transfers between devices with their start and end apart: 18, of which 7 were waited for; matrix products, arithmetic and copies ran while one was open for 36% of the time, Pallas kernels for 0%

profile of v1, /device:TPU:0, one launch (start us, length us, event | category | flops | bytes accessed | tf_op | source)
XLA Modules:
  0.0 786.5 jit_solution(13005885202175331573)
XLA Ops:
  51.8 5.6 collective-permute-start.7
  59.4 5.7 maximum_bitcast_fusion
  65.1 7.8 copy.231
  89.7 5.9 copy.232
  99.5 8.6 %fusion.50 = f32[2,16,8,17,64]{4,2,3,1,0:T(8,128)S(1)} fusion(bf16[3,3,3,64,64]{4,3,2,1,0:T(8,128)(2,1)S(1)} %copy-done.33, bf16[64,4,18,1,7,2]{0,4,5,2,1,3:T(8,128)(2,1)S(1)} %slice.228, bf16[64,4,18,1,8,17]{0,4,5,2,1,3:T(8,128)(2,1)S(1)} %copy.170, pred[8,17]{0,1:T(8,128)(4,1)S(1)} %copy-done.44), kind=kOutput, calls=%fused_computation.57 | convolution fusion | flops 967073792 | bytes 2717832 | tf_op jit(solution)/shard_map/conv_general_dilated | solution.py:39
  116.8 5.2 fusion.139
  125.0 9.1 %copy.202 = bf16[1,64,4,18,130]{1,0,4,3,2:T(2,128)(2,1)} copy(bf16[1,64,4,18,130]{4,1,3,2,0:T(8,128)(2,1)S(1)} %copy-done.12) | data formatting | bytes 2396160 | tf_op jit(solution)/shard_map/broadcast_in_dim | solution.py:40
  135.0 5.6 collective-permute-start.11
  148.4 30.6 %convolution_convert_fusion.1 = bf16[3,3,3,64,64]{3,4,2,1,0:T(8,128)(2,1)} fusion(bf16[1,64,4,18,130]{1,0,4,3,2:T(2,128)(2,1)S(1)} %copy-done.15, bf16[64,1,2,16,128]{0,1,4,3,2:T(2,128)(2,1)S(1)} %copy-done.24), kind=kOutput, calls=%fused_computation.66 | convolution fusion | flops 906080256 | bytes 1943552 | tf_op jit(solution)/shard_map/transpose | solution.py:74
  179.0 5.2 maximum_bitcast_fusion.1
  188.2 5.7 copy.233
  198.9 5.6 collective-permute-start.5
  208.7 9.4 %copy.208 = bf16[1,64,4,18,130]{1,0,4,3,2:T(2,128)(2,1)} copy(bf16[1,64,4,18,130]{4,1,3,2,0:T(8,128)(2,1)S(1)} %maximum_bitcast_fusion.4) | data formatting | bytes 2396160 | tf_op jit(solution)/shard_map/broadcast_in_dim | solution.py:67
  218.0 32.9 %convolution_convert_fusion = bf16[3,3,3,64,64]{3,4,2,1,0:T(8,128)(2,1)S(1)} fusion(bf16[1,64,4,18,130]{1,0,4,3,2:T(2,128)(2,1)} %copy.208, bf16[64,1,2,16,128]{0,1,4,3,2:T(2,128)(2,1)} %copy.209), kind=kOutput, calls=%fused_computation.65 | convolution fusion | flops 906080256 | bytes 1943552 | tf_op jit(solution)/shard_map/transpose | solution.py:74
  265.7 72.5 %all-reduce.11.cloned.1.call-done = bf16[8,2,27,512]{3,1,2,0:T(2,128)(2,1)} async-done(((bf16[8,2,27,512]{3,1,2,0:T(2,128)(2,1)}), bf16[8,2,27,512]{3,1,2,0:T(2,128)(2,1)}) %all-reduce.11.cloned.1.call-update) | async-done | bytes 442384
  340.4 116.6 %all-reduce.7.cloned.1.call-done = bf16[12,27,512]{2,1,0:T(8,128)(2,1)} async-done(((bf16[12,27,512]{2,1,0:T(8,128)(2,1)}), bf16[12,27,512]{2,1,0:T(8,128)(2,1)}) %all-reduce.7.cloned.1.call-update) | async-done | bytes 331792 | tf_op jit(solution)/shard_map/psum | solution.py:146
  460.0 5.4 select_convert_fusion
  466.6 112.2 %all-reduce.13.cloned.1.call-done = (bf16[1,2,27,512]{3,2,1,0:T(8,128)(2,1)}, bf16[2,27,512]{2,1,0:T(8,128)(2,1)}) async-done(((bf16[1,2,27,512]{3,2,1,0:T(8,128)(2,1)}, bf16[2,27,512]{2,1,0:T(8,128)(2,1)}), (bf16[1,2,27,512]{3,2,1,0:T(8,128)(2,1)}, bf16[2,27,512]{2,1,0:T(8,128)(2,1)})) %all-reduce.13.cloned.1.call-update) | async-done | bytes 110608 | tf_op jit(solution)/shard_map/psum | solution.py:150
  582.4 34.9 %all_gather.13 = bf16[8,2,27,512]{3,1,2,0:T(2,128)(2,1)S(1)} all-gather(bf16[1,2,27,512]{3,1,2,0:T(2,128)(2,1)S(1)} %copy.188), channel_id=1, replica_groups=mesh['dp'=16,'space'=8] {'space'}, dimensions={0}, use_global_device_ids=true | all-gather | bytes 497664 | tf_op jit(solution)/shard_map/all_gather | solution.py:88
  618.2 79.7 %all-reduce.9.cloned.1.call-done = bf16[1,10,27,512]{3,2,1,0:T(8,128)(2,1)} async-done(((bf16[1,10,27,512]{3,2,1,0:T(8,128)(2,1)}), bf16[1,10,27,512]{3,2,1,0:T(8,128)(2,1)}) %all-reduce.9.cloned.1.call-update) | async-done | bytes 276496 | tf_op jit(solution)/shard_map/psum | solution.py:167
  697.9 10.3 %fusion.47 = f32[2,16,8,17,64]{4,2,3,1,0:T(8,128)S(1)} fusion(bf16[3,3,3,64,64]{4,3,2,1,0:T(8,128)(2,1)S(1)} %reshape_reshape_squeeze.15, bf16[64,4,18,1,7,2]{0,4,5,2,1,3:T(8,128)(2,1)S(1)} %copy-done.35, bf16[64,4,18,1,8,17]{0,4,5,2,1,3:T(8,128)(2,1)} %copy-done.22, pred[8,17]{0,1:T(8,128)(4,1)S(1)} %copy-done.45), kind=kOutput, calls=%fused_computation.56 | convolution fusion | flops 967073792 | bytes 2717832 | tf_op jit(solution)/shard_map/conv_general_dilated | solution.py:39
  736.5 4.8 copy.235
  742.9 8.6 %fusion.42 = f32[2,16,8,17,64]{4,2,3,1,0:T(8,128)S(1)} fusion(bf16[3,3,3,64,64]{4,3,2,1,0:T(8,128)(2,1)S(1)} %reshape_reshape_squeeze.16, bf16[64,4,18,1,7,2]{0,4,5,2,1,3:T(8,128)(2,1)S(1)} %slice.252, bf16[64,4,18,1,8,17]{0,4,5,2,1,3:T(8,128)(2,1)S(1)} %copy.197, pred[8,17]{0,1:T(8,128)(4,1)S(1)} %copy-done.45), kind=kOutput, calls=%fused_computation.55 | convolution fusion | flops 967073792 | bytes 2717832 | tf_op jit(solution)/shard_map/conv_general_dilated | solution.py:39
  755.0 10.5 %all-gather.2.cloned.1.call-done = bf16[8,10,27,512]{3,2,1,0:T(8,128)(2,1)} async-done(((bf16[1,10,27,512]{3,2,1,0:T(8,128)(2,1)}), bf16[8,10,27,512]{3,2,1,0:T(8,128)(2,1)}) %all-gather.2.cloned.1.call-update) | async-done | bytes 2211856 | tf_op jit(solution)/shard_map/all_gather | solution.py:88
  (256 shorter events, 172.5 us)
Async XLA Ops:
  7.2 247.8 %reduce-scatter.2.cloned.1.call-start = ((), (), s32[]{:S(2)}) async-start(), calls=%async_computation.1 | async-start | bytes 3538944 | tf_op jit(solution)/shard_map/reduce_scatter | solution.py:82
  9.1 42.8 %collective-permute-start = (bf16[64,1,16,128]{3,2,1,0:T(8,128)(2,1)}, bf16[64,1,16,128]{3,2,1,0:T(8,128)(2,1)S(1)}, u32[]{:S(2)}, u32[]{:S(2)}) collective-permute-start(bf16[64,1,16,128]{3,2,1,0:T(8,128)(2,1)} %get-tuple-element.78), channel_id=1, source_target_pairs={{0,1},{1,2},{2,3},{3,4},{4,5},{5,6},{6,7},{7,0},{8,9},{9,10},{10,1... | collective-permute-start | bytes 786440 | tf_op jit(solution)/shard_map/ppermute | solution.py:23
  12.4 45.1 %collective-permute-start.1 = (bf16[64,1,16,128]{3,2,1,0:T(8,128)(2,1)}, bf16[64,1,16,128]{3,2,1,0:T(8,128)(2,1)S(1)}, u32[]{:S(2)}, u32[]{:S(2)}) collective-permute-start(bf16[64,1,16,128]{3,2,1,0:T(8,128)(2,1)} %get-tuple-element.79), channel_id=1, source_target_pairs={{1,0},{2,1},{3,2},{4,3},{5,4},{6,5},{7,6},{0,7},{9,8},{10,9},{11,1... | collective-permute-start | bytes 786440 | tf_op jit(solution)/shard_map/ppermute | solution.py:26
  16.8 65.7 %collective-permute-start.2 = (bf16[64,1,16,128]{3,0,2,1:T(8,128)(2,1)}, bf16[64,1,16,128]{3,0,2,1:T(8,128)(2,1)}, u32[]{:S(2)}, u32[]{:S(2)}) collective-permute-start(bf16[64,1,16,128]{3,0,2,1:T(8,128)(2,1)} %get-tuple-element.76), channel_id=1, source_target_pairs={{0,1},{1,2},{2,3},{3,4},{4,5},{5,6},{6,7},{7,0},{8,9},{9,10},{10,1... | collective-permute-start | bytes 786440 | tf_op jit(solution)/shard_map/ppermute | solution.py:23
  18.0 64.5 %collective-permute-start.3 = (bf16[64,1,16,128]{3,0,2,1:T(8,128)(2,1)}, bf16[64,1,16,128]{3,0,2,1:T(8,128)(2,1)}, u32[]{:S(2)}, u32[]{:S(2)}) collective-permute-start(bf16[64,1,16,128]{3,0,2,1:T(8,128)(2,1)} %get-tuple-element.77), channel_id=1, source_target_pairs={{1,0},{2,1},{3,2},{4,3},{5,4},{6,5},{7,6},{0,7},{9,8},{10,9},{11,1... | collective-permute-start | bytes 786440 | tf_op jit(solution)/shard_map/ppermute | solution.py:26
  31.7 306.6 %all-reduce.11.cloned.1.call-start = ((), (), s32[]{:S(2)}) async-start(), calls=%async_computation.5 | async-start | bytes 884736
  33.5 107.1 %collective-permute-start.6 = (bf16[64,1,16,128]{3,2,1,0:T(8,128)(2,1)}, bf16[64,1,16,128]{3,2,1,0:T(8,128)(2,1)}, u32[]{:S(2)}, u32[]{:S(2)}) collective-permute-start(bf16[64,1,16,128]{3,2,1,0:T(8,128)(2,1)} %get-tuple-element.70), channel_id=1, source_target_pairs={{0,1},{1,2},{2,3},{3,4},{4,5},{5,6},{6,7},{7,0},{8,9},{9,10},{10,1... | collective-permute-start | bytes 786440 | tf_op jit(solution)/shard_map/ppermute | solution.py:23
  51.8 88.8 %collective-permute-start.7 = (bf16[64,1,16,128]{3,2,1,0:T(8,128)(2,1)}, bf16[64,1,16,128]{3,2,1,0:T(8,128)(2,1)}, u32[]{:S(2)}, u32[]{:S(2)}) collective-permute-start(bf16[64,1,16,128]{3,2,1,0:T(8,128)(2,1)} %get-tuple-element.71), channel_id=1, source_target_pairs={{1,0},{2,1},{3,2},{4,3},{5,4},{6,5},{7,6},{0,7},{9,8},{10,9},{11,1... | collective-permute-start | bytes 786440 | tf_op jit(solution)/shard_map/ppermute | solution.py:26
  135.0 69.5 %collective-permute-start.10 = (bf16[64,1,16,128]{3,2,1,0:T(8,128)(2,1)}, bf16[64,1,16,128]{3,2,1,0:T(8,128)(2,1)}, u32[]{:S(2)}, u32[]{:S(2)}) collective-permute-start(bf16[64,1,16,128]{3,2,1,0:T(8,128)(2,1)} %get-tuple-element.72), channel_id=1, source_target_pairs={{0,1},{1,2},{2,3},{3,4},{4,5},{5,6},{6,7},{7,0},{8,9},{9,10},{10,1... | collective-permute-start | bytes 786440 | tf_op jit(solution)/shard_map/ppermute | solution.py:23
  135.0 69.5 %collective-permute-start.11 = (bf16[64,1,16,128]{3,2,1,0:T(8,128)(2,1)}, bf16[64,1,16,128]{3,2,1,0:T(8,128)(2,1)}, u32[]{:S(2)}, u32[]{:S(2)}) collective-permute-start(bf16[64,1,16,128]{3,2,1,0:T(8,128)(2,1)} %get-tuple-element.73), channel_id=1, source_target_pairs={{1,0},{2,1},{3,2},{4,3},{5,4},{6,5},{7,6},{0,7},{9,8},{10,9},{11,1... | collective-permute-start | bytes 786440 | tf_op jit(solution)/shard_map/ppermute | solution.py:26
  198.9 53.8 %collective-permute-start.4 = (bf16[64,1,16,128]{3,2,1,0:T(8,128)(2,1)}, bf16[64,1,16,128]{3,2,1,0:T(8,128)(2,1)}, u32[]{:S(2)}, u32[]{:S(2)}) collective-permute-start(bf16[64,1,16,128]{3,2,1,0:T(8,128)(2,1)} %get-tuple-element.74), channel_id=1, source_target_pairs={{0,1},{1,2},{2,3},{3,4},{4,5},{5,6},{6,7},{7,0},{8,9},{9,10},{10,1... | collective-permute-start | bytes 786440 | tf_op jit(solution)/shard_map/ppermute | solution.py:23
  198.9 53.8 %collective-permute-start.5 = (bf16[64,1,16,128]{3,2,1,0:T(8,128)(2,1)}, bf16[64,1,16,128]{3,2,1,0:T(8,128)(2,1)}, u32[]{:S(2)}, u32[]{:S(2)}) collective-permute-start(bf16[64,1,16,128]{3,2,1,0:T(8,128)(2,1)} %get-tuple-element.75), channel_id=1, source_target_pairs={{1,0},{2,1},{3,2},{4,3},{5,4},{6,5},{7,6},{0,7},{9,8},{10,9},{11,1... | collective-permute-start | bytes 786440 | tf_op jit(solution)/shard_map/ppermute | solution.py:26
  254.1 202.9 %all-reduce.7.cloned.1.call-start = ((), (), s32[]{:S(2)}) async-start(), calls=%async_computation.2 | async-start | bytes 786432 | tf_op jit(solution)/shard_map/psum | solution.py:146
  255.0 323.9 %all-reduce.13.cloned.1.call-start = ((), (), s32[]{:S(2)}) async-start(), calls=%async_computation.6 | async-start | bytes 262144 | tf_op jit(solution)/shard_map/psum | solution.py:150
  264.5 193.5 %copy-start.31 = (f32[2,27,512]{2,0,1:T(2,128)S(1)}, f32[2,27,512]{2,0,1:T(2,128)}, u32[]{:S(2)}) copy-start(f32[2,27,512]{2,0,1:T(2,128)} %gather_fusion.2) | copy-start | bytes 331780
  264.6 193.5 %copy-start.32 = (f32[2,27,512]{2,0,1:T(2,128)S(1)}, f32[2,27,512]{2,0,1:T(2,128)}, u32[]{:S(2)}) copy-start(f32[2,27,512]{2,0,1:T(2,128)} %gather_fusion.3) | copy-start | bytes 331780
  264.6 193.5 %copy-start.40 = (pred[2]{0:T(512)(128)(4,1)S(1)}, pred[2]{0:T(512)(128)(4,1)}, u32[]{:S(2)}) copy-start(pred[2]{0:T(512)(128)(4,1)} %get-tuple-element.39) | copy-start | bytes 10
  264.6 193.5 %copy-start.41 = (pred[2]{0:T(512)(128)(4,1)S(1)}, pred[2]{0:T(512)(128)(4,1)}, u32[]{:S(2)}) copy-start(pred[2]{0:T(512)(128)(4,1)} %fusion.99) | copy-start | bytes 10
  264.9 195.0 %copy-start.45 = (pred[8,17]{0,1:T(8,128)(4,1)S(1)}, pred[8,17]{0,1:T(8,128)(4,1)}, u32[]{:S(2)}) copy-start(pred[8,17]{0,1:T(8,128)(4,1)} %constant.141) | copy-start | bytes 412
  459.9 238.0 %all-reduce.9.cloned.1.call-start = ((), (), s32[]{:S(2)}) async-start(), calls=%async_computation.3 | async-start | bytes 655360 | tf_op jit(solution)/shard_map/psum | solution.py:167
  581.4 116.6 %copy-start.35 = (bf16[64,4,18,1,7,2]{0,4,5,2,1,3:T(8,128)(2,1)S(1)}, bf16[64,4,18,1,7,2]{0,4,5,2,1,3:T(8,128)(2,1)}, u32[]{:S(2)}) copy-start(bf16[64,4,18,1,7,2]{0,4,5,2,1,3:T(8,128)(2,1)} %slice.242) | copy-start | bytes 387076
  582.2 183.3 %all-gather.2.cloned.1.call-start = ((), (), s32[]{:S(2)}) async-start(), calls=%async_computation.4 | async-start | bytes 2949120 | tf_op jit(solution)/shard_map/all_gather | solution.py:88
  713.4 14.5 %collective-permute-start.8 = (bf16[64,1,16,128]{3,2,1,0:T(8,128)(2,1)}, bf16[64,1,16,128]{3,2,1,0:T(8,128)(2,1)}, u32[]{:S(2)}, u32[]{:S(2)}) collective-permute-start(bf16[64,1,16,128]{3,2,1,0:T(8,128)(2,1)} %get-tuple-element.68), channel_id=1, source_target_pairs={{0,1},{1,2},{2,3},{3,4},{4,5},{5,6},{6,7},{7,0},{8,9},{9,10},{10,1... | collective-permute-start | bytes 786440 | tf_op jit(solution)/shard_map/ppermute | solution.py:23
  716.2 14.8 %collective-permute-start.9 = (bf16[64,1,16,128]{3,2,1,0:T(8,128)(2,1)S(1)}, bf16[64,1,16,128]{3,2,1,0:T(8,128)(2,1)}, u32[]{:S(2)}, u32[]{:S(2)}) collective-permute-start(bf16[64,1,16,128]{3,2,1,0:T(8,128)(2,1)S(1)} %get-tuple-element.69), channel_id=1, source_target_pairs={{1,0},{2,1},{3,2},{4,3},{5,4},{6,5},{7,6},{0,7},{9,8},{10,9},{11,1... | collective-permute-start | bytes 786440 | tf_op jit(solution)/shard_map/ppermute | solution.py:26
  (40 other events, 987.6 us)
Sparse Core Ops, SparseCore 0:
  31.8 85.4 reduce-scatter.1
  254.2 83.9 all-reduce.10
  340.7 116.2 all-reduce.6
  460.0 118.7 all-reduce.12
  582.3 115.5 all-reduce.8
  700.1 65.3 all-gather.1
